TPU v7x, 256 devices: a whole 4x4x8 slice. The times are simulated.
256 devices in a mesh: graph: 8 (over z), index: 32 (over x, y, core).
Axes of the slice: x: 4, y: 4, z: 8, core: 2. Of those that a mesh axis runs over, the one named last changes fastest.
Arguments:
- features: bfloat16 [65536, 1024], P(('graph', 'index')), may hold values from -6 to 6
- q_weight: bfloat16 [1024, 1024], replicated, may hold values from -0.1875 to 0.1875
- q_bias: float32 [1024], replicated, may hold values from -3 to 3
- w_self: bfloat16 [1024, 1024], replicated, may hold values from -0.125 to 0.125
- w_neigh: bfloat16 [1024, 1024], replicated, may hold values from -0.125 to 0.125
- z_bias: float32 [1024], replicated, may hold values from -3 to 3
- centroids: bfloat16 [8192, 1024], P('index'), may hold values from -0.1875 to 0.1875
- requests: int32 [256, 32, 16], P(('graph', 'index')), may hold values from 0 to 255, as said below
- slots: int32 [65536, 50], P(('graph', 'index')), may hold values from 0 to 511
- importance: float32 [65536, 50], P(('graph', 'index')), may hold values from 0.1 to 10
- labels: int32 [65536, 1], P(('graph', 'index')), may hold values from 0 to 31; in each aligned block of 256 rows (0 to 255, 256 to 511, ...) at most 16 rows name the same one
Outputs:
- scores: bfloat16 [65536, 256], P(('graph', 'index'))
Inputs may be any that keep to these rules, and one draw needn't show every extreme that they name: `requests`: the 16 rows that a device asks of one device are distinct. `labels`: the rows of one device carry any one label at most 16 times.
All inputs are finite; a program needn't handle non-finite values.
Results may differ from a plain program's by a relative error of at most 0.0051.
Values may be sent and summed in bfloat16 or wider, within the bound.
No kernel may reach another device: no remote copies, remote signals or barrier semaphores. Data moves between devices by JAX's collectives and lax.ppermute only.
A program may use at most 64 MiB of HBM per device.

v0:
```python
import jax
import jax.numpy as jnp
from jax import lax
from jax.sharding import PartitionSpec as P


def place_rows(label_rows, peer_count, owner_slots):
    hits = (label_rows[:, None] == jnp.arange(peer_count, dtype=jnp.int32)[None, :]).astype(
        jnp.int32
    )
    ranks = jnp.sum(hits * (jnp.cumsum(hits, axis=0) - 1), axis=1)
    return label_rows * owner_slots + ranks


def one_hot(index, count):
    return (index[:, None] == jnp.arange(count, dtype=jnp.int32)[None, :]).astype(jnp.bfloat16)


def body(
    features,
    q_weight,
    q_bias,
    w_self,
    w_neigh,
    z_bias,
    centroids,
    requests,
    slots,
    importance,
    labels,
):
    row_count = features.shape[0]
    width = features.shape[1]
    peer_count = lax.axis_size("index")
    owner_slots = max(2 * row_count // peer_count, 2)
    fetch_slots = requests.shape[2]
    slot_count = peer_count * fetch_slots
    cent_count = centroids.shape[0]
    me = lax.axis_index("index")
    own_rows = jnp.where(
        jnp.arange(peer_count, dtype=jnp.int32)[:, None, None] == me,
        requests.astype(jnp.float32),
        0.0,
    )
    all_requests = lax.psum(own_rows, "index")
    wanted = lax.dynamic_index_in_dim(all_requests, me, axis=1, keepdims=False).astype(jnp.int32)
    messages = jax.nn.relu(
        jnp.dot(features, q_weight, preferred_element_type=jnp.float32) + q_bias
    ).astype(jnp.bfloat16)
    weights_norm = importance / jnp.sum(importance, axis=1, keepdims=True)
    slot_ids = jnp.arange(slot_count, dtype=jnp.int32)
    mixing = jnp.sum(
        jnp.where(slots[:, :, None] == slot_ids[None, None, :], weights_norm[:, :, None], 0.0),
        axis=1,
    ).astype(jnp.bfloat16)
    outgoing_msgs = jnp.dot(
        one_hot(wanted.reshape(-1), row_count),
        lax.optimization_barrier(messages),
        preferred_element_type=jnp.float32,
    ).astype(jnp.bfloat16)
    fetched = lax.all_to_all(
        outgoing_msgs.reshape(peer_count, fetch_slots, width),
        "index",
        split_axis=0,
        concat_axis=0,
        tiled=True,
    ).reshape(slot_count, width)
    pooled = jnp.dot(mixing, fetched, preferred_element_type=jnp.float32).astype(jnp.bfloat16)
    hidden = jax.nn.relu(
        jnp.dot(features, w_self, preferred_element_type=jnp.float32)
        + jnp.dot(pooled, w_neigh, preferred_element_type=jnp.float32)
        + z_bias
    )
    normed = (hidden * lax.rsqrt(jnp.mean(hidden * hidden, axis=1, keepdims=True) + 1e-06)).astype(
        jnp.bfloat16
    )
    positions = place_rows(labels[:, 0], peer_count, owner_slots)
    pick = one_hot(positions, peer_count * owner_slots)
    outgoing = lax.dot_general(
        pick, normed, (((0,), (0,)), ((), ())), preferred_element_type=jnp.float32
    ).astype(jnp.bfloat16)
    outgoing = outgoing.reshape(peer_count, owner_slots, width)
    arrived = lax.all_to_all(outgoing, "index", split_axis=0, concat_axis=0, tiled=True)
    flat_rows = arrived.reshape(-1, width)
    raw_scores = lax.dot_general(
        flat_rows, centroids, (((1,), (1,)), ((), ())), preferred_element_type=jnp.float32
    ).astype(jnp.bfloat16)
    returned = lax.all_to_all(
        raw_scores.reshape(peer_count, arrived.shape[1], cent_count),
        "index",
        split_axis=0,
        concat_axis=0,
        tiled=True,
    )
    return jnp.dot(
        pick,
        returned.reshape(peer_count * owner_slots, cent_count),
        preferred_element_type=jnp.float32,
    ).astype(jnp.bfloat16)


def solution(mesh):
    return jax.shard_map(
        body,
        mesh=mesh,
        in_specs=(
            P(("graph", "index"), None),
            P(),
            P(),
            P(),
            P(),
            P(),
            P("index", None),
            P(("graph", "index"), None, None),
            P(("graph", "index"), None),
            P(("graph", "index"), None),
            P(("graph", "index"), None),
        ),
        out_specs=P(("graph", "index"), None),
        check_vma=False,
    )
```

profile of v0, /device:TPU:1, one launch (start us, length us, event | category | flops | bytes accessed | tf_op | source)
XLA Modules:
  0.0 201.9 jit_solution(17790053467064373194)
XLA Ops:
  6.5 0.8 convert_bitcast_fusion
  7.4 0.1 copy.20
  7.5 0.9 broadcast_select_fusion
  8.4 0.0 all-reduce.2.cloned.1.call-update
  8.4 0.7 fusion.12
  9.1 0.6 reduce-window.6
  9.7 0.2 slice_reduce_fusion
  9.9 2.6 %fusion.13 = f32[256,1024]{1,0:T(8,128)S(1)} fusion(bf16[256,1024]{1,0:T(8,128)(2,1)} %param.11, bf16[1024,1024]{1,0:T(8,128)(2,1)} %param.14), kind=kOutput, calls=%fused_computation.37 | convolution fusion | flops 536870912 | bytes 3670016 | tf_op jit(solution)/shard_map/dot_general | solution.py:70
  12.6 0.0 copy-start.3
  12.6 2.6 %fusion.3 = bf16[256,1024]{1,0:T(8,128)(2,1)} fusion(bf16[256,1024]{1,0:T(8,128)(2,1)} %param.11, bf16[1024,1024]{1,0:T(8,128)(2,1)S(1)} %copy-done.4, f32[1024]{0:T(1024)S(1)} %copy-done.6), kind=kOutput, calls=%fused_computation.9 | convolution fusion | flops 537657344 | bytes 3149824 | tf_op jit(solution)/shard_map/dot_general | solution.py:48
  15.1 0.1 fusion.11
  15.2 113.5 %all-reduce.2.cloned.1.call-done = f32[32,32,16]{2,0,1:T(8,128)} async-done(((f32[32,32,16]{2,0,1:T(8,128)}), f32[32,32,16]{2,0,1:T(8,128)}) %all-reduce.2.cloned.1.call-update) | async-done | bytes 65552 | tf_op jit(solution)/shard_map/psum | solution.py:45
  128.7 0.7 dynamic-slice_convert_fusion
  129.4 0.1 convert_element_type.48
  129.5 2.6 %convolution_convert_fusion.1 = bf16[512,1024]{1,0:T(8,128)(2,1)} fusion(bf16[256,1024]{1,0:T(8,128)(2,1)} %fusion.3, s32[512]{0:T(512)S(1)} %convert_element_type.48), kind=kOutput, calls=%fused_computation.3 | convolution fusion | flops 269090816 | bytes 1574912 | tf_op jit(solution)/shard_map/dot_general | solution.py:56
  132.1 6.1 %all-to-all-start = ((bf16[32,16,1024]{2,1,0:T(8,128)(2,1)}), bf16[32,16,1024]{2,1,0:T(8,128)(2,1)}, u32[]{:S(2)}, u32[]{:S(2)}) async-start(bf16[32,16,1024]{2,1,0:T(8,128)(2,1)} %bitcast.6), calls=%async_computation | async-start | bytes 2097152 | tf_op jit(solution)/shard_map/all_to_all | solution.py:61
  138.3 4.3 %select_reduce_fusion = bf16[256,512]{1,0:T(8,128)(2,1)S(1)} fusion(f32[256,50]{0,1:T(8,128)S(1)} %broadcast_divide_fusion, s32[256,50]{0,1:T(8,128)S(1)} %copy-done.2), kind=kLoop, calls=%fused_computation | loop fusion | flops 19529728 | bytes 364544 | tf_op jit(solution)/shard_map/reduce_sum | solution.py:52
  142.6 12.5 %all-to-all-done = bf16[32,16,1024]{2,1,0:T(8,128)(2,1)} async-done(((bf16[32,16,1024]{2,1,0:T(8,128)(2,1)}), bf16[32,16,1024]{2,1,0:T(8,128)(2,1)}, u32[]{:S(2)}, u32[]{:S(2)}) %all-to-all-start) | async-done | bytes 1048608 | tf_op jit(solution)/shard_map/all_to_all | solution.py:61
  155.2 3.3 %multiply_reduce_fusion = (f32[256]{0:T(256)S(1)}, f32[256,1024]{1,0:T(8,128)}) fusion(f32[1024]{0:T(1024)S(1)} %copy-done.7, f32[256,1024]{1,0:T(8,128)S(1)} %fusion.13, bf16[1024,1024]{1,0:T(8,128)(2,1)S(1)} %copy-done, bf16[512,1024]{1,0:T(8,128)(2,1)} %bitcast.7, bf16[256,512]{1,0:T(8,128)(2,1)S(1)} %select_reduce_fusion), kind=kOutput, calls=%fused_computation.14 | convolution fusion | flops 806878976 | bytes 5510144 | tf_op jit(solution)/shard_map/dot_general | solution.py:71
  158.4 1.8 convolution_convert_fusion
  160.3 20.6 %all_to_all.15 = bf16[32,16,1024]{2,1,0:T(8,128)(2,1)S(1)} all-to-all(bf16[32,16,1024]{2,1,0:T(8,128)(2,1)S(1)} %bitcast.40), channel_id=1, replica_groups=mesh['graph'=8,'index'=32] {'index'}, dimensions={0} | all-to-all | bytes 2097152 | tf_op jit(solution)/shard_map/all_to_all | solution.py:83
  180.9 0.5 convolution_convert_fusion.3
  181.4 12.7 %all_to_all.16 = bf16[32,16,256]{2,1,0:T(8,128)(2,1)S(1)} all-to-all(bf16[32,16,256]{2,1,0:T(8,128)(2,1)S(1)} %bitcast.43), channel_id=1, replica_groups=mesh['graph'=8,'index'=32] {'index'}, dimensions={0} | all-to-all | bytes 524288 | tf_op jit(solution)/shard_map/all_to_all | solution.py:88
  194.1 0.9 convolution_convert_fusion.4
  (23 shorter events, 0.1 us)
Async XLA Ops:
  6.5 148.6 %copy-start = (bf16[1024,1024]{1,0:T(8,128)(2,1)S(1)}, bf16[1024,1024]{1,0:T(8,128)(2,1)}, u32[]{:S(2)}) copy-start(bf16[1024,1024]{1,0:T(8,128)(2,1)} %param.15) | copy-start | bytes 6291460
  6.5 122.2 %all-reduce.2.cloned.1.call-start = ((), (), s32[]{:S(2)}) async-start(), calls=%async_computation.3 | async-start | bytes 1048576 | tf_op jit(solution)/shard_map/psum | solution.py:45
  8.4 4.1 %copy-start.6 = (f32[1024]{0:T(1024)S(1)}, f32[1024]{0:T(1024)}, u32[]{:S(2)}) copy-start(f32[1024]{0:T(1024)} %param.13) | copy-start | bytes 12292
  9.9 2.6 %copy-start.4 = (bf16[1024,1024]{1,0:T(8,128)(2,1)S(1)}, bf16[1024,1024]{1,0:T(8,128)(2,1)}, u32[]{:S(2)}) copy-start(bf16[1024,1024]{1,0:T(8,128)(2,1)} %param.12) | copy-start | bytes 6291460
  12.6 2.6 %copy-start.3 = (s32[256,1]{0,1:T(1,128)S(1)}, s32[256,1]{0,1:T(1,128)}, u32[]{:S(2)}) copy-start(s32[256,1]{0,1:T(1,128)} %param.21) | copy-start | bytes 3076
  15.1 123.1 %copy-start.1 = (f32[256,50]{0,1:T(8,128)S(1)}, f32[256,50]{0,1:T(8,128)}, u32[]{:S(2)}) copy-start(f32[256,50]{0,1:T(8,128)} %param.20) | copy-start | bytes 153604
  15.1 123.1 %copy-start.2 = (s32[256,50]{0,1:T(8,128)S(1)}, s32[256,50]{0,1:T(8,128)}, u32[]{:S(2)}) copy-start(s32[256,50]{0,1:T(8,128)} %param.19) | copy-start | bytes 153604
  129.5 25.6 %copy-start.7 = (f32[1024]{0:T(1024)S(1)}, f32[1024]{0:T(1024)}, u32[]{:S(2)}) copy-start(f32[1024]{0:T(1024)} %param.16) | copy-start | bytes 12292
  132.1 23.0 %all-to-all-start = ((bf16[32,16,1024]{2,1,0:T(8,128)(2,1)}), bf16[32,16,1024]{2,1,0:T(8,128)(2,1)}, u32[]{:S(2)}, u32[]{:S(2)}) async-start(bf16[32,16,1024]{2,1,0:T(8,128)(2,1)} %bitcast.6), calls=%async_computation | async-start | bytes 2097152 | tf_op jit(solution)/shard_map/all_to_all | solution.py:61
  158.4 22.5 %copy-start.5 = (bf16[256,1024]{1,0:T(8,128)(2,1)S(1)}, bf16[256,1024]{1,0:T(8,128)(2,1)}, u32[]{:S(2)}) copy-start(bf16[256,1024]{1,0:T(8,128)(2,1)} %param.17) | copy-start | bytes 1572868
Sparse Core Ops, SparseCore 0:
  10.5 118.1 all-reduce.1
where the time goes:
time: 202 us
  waiting for transfers between devices  126 us (62%)
  blocking collectives  33.3 us (16%)
  matrix products  14.3 us (7%)
  between operations  13.5 us (7%)
  other arithmetic  8.31 us (4%)
  starting transfers between devices  6.08 us (3%)
    psum x1, waiting for transfers between devices, body(): all_requests = lax.psum(own_rows, 'index')  113 us
    all_to_all x1, blocking collectives, body(): lax.all_to_all(outgoing, 'index', split_axis=0, concat_axis=0, tiled=True)  20.6 us
    all_to_all x1, blocking collectives, body(): lax.all_to_all(raw_scores.reshape(peer_count, arrived.shape[1], cent_coun...  12.7 us
    all_to_all x1, waiting for transfers between devices, body(): lax.all_to_all(outgoing_msgs.reshape(peer_count, fetch_slots, width), 'in...  12.5 us
    all_to_all x1, starting transfers between devices, body(): lax.all_to_all(outgoing_msgs.reshape(peer_count, fetch_slots, width), 'in...  6.08 us
    reduce_sum x1, other arithmetic, body(): jnp.sum(jnp.where(slots[:, :, None] == slot_ids[None, None, :], weights_n...  4.35 us
  transfers between devices with their start and end apart: 2, of which 2 were waited for; matrix products, arithmetic and copies ran while one was open for 6% of the time, Pallas kernels for 0%

commit v1 on v0

--- a/solution.py
+++ b/solution.py
@@ -42,7 +42,13 @@
         requests.astype(jnp.float32),
         0.0,
     )
-    all_requests = lax.psum(own_rows, "index")
+    extent = jax.lax.axis_size("index")
+    all_requests = own_rows
+    for k0 in [
+        [(q, q ^ dev_j) for q in range(extent)] for dev_j in (1, 2, 4, 8, 16) if dev_j < extent
+    ]:
+        earlier = jax.lax.ppermute(all_requests, "index", k0)
+        all_requests = all_requests + earlier
     wanted = lax.dynamic_index_in_dim(all_requests, me, axis=1, keepdims=False).astype(jnp.int32)
     messages = jax.nn.relu(
         jnp.dot(features, q_weight, preferred_element_type=jnp.float32) + q_bias

time: 202 us -> 130 us (0.64)
  waiting for transfers between devices: 126 us -> 59.1 us
  between operations: 13.5 us -> 0.2 us
  starting transfers between devices: 6.08 us -> 15 us
    psum x1 -> x0, waiting for transfers between devices: 113 us -> none  [body(): all_requests = lax.psum(own_rows, 'index')]
    ppermute x0 -> x5, waiting for transfers between devices: none -> 46.5 us  [body(): earlier = jax.lax.ppermute(all_requests, 'index', k0)]
    ppermute x0 -> x5, starting transfers between devices: none -> 5.93 us  [body(): earlier = jax.lax.ppermute(all_requests, 'index', k0)]
    all_to_all x1, starting transfers between devices: 6.08 us -> 9.03 us  [body(): lax.all_to_all(outgoing_msgs.reshape(peer_count, fetch_slots, width), 'in...]
  transfers between devices with their start and end apart: 2 -> 6, of which waited for: 2 -> 5; matrix products, arithmetic and copies ran while one was open for 6% -> 8% of each run, Pallas kernels for 0% -> 0%
where the time goes in v1:
time: 130 us
  waiting for transfers between devices  59.1 us (45%)
  blocking collectives  33.3 us (26%)
  starting transfers between devices  15 us (12%)
  matrix products  14.1 us (11%)
  other arithmetic  7.6 us (6%)
    ppermute x5, waiting for transfers between devices, body(): earlier = jax.lax.ppermute(all_requests, 'index', k0)  46.5 us
    all_to_all x1, blocking collectives, body(): lax.all_to_all(outgoing, 'index', split_axis=0, concat_axis=0, tiled=True)  20.6 us
    all_to_all x1, blocking collectives, body(): lax.all_to_all(raw_scores.reshape(peer_count, arrived.shape[1], cent_coun...  12.7 us
    all_to_all x1, waiting for transfers between devices, body(): lax.all_to_all(outgoing_msgs.reshape(peer_count, fetch_slots, width), 'in...  12.5 us
    all_to_all x1, starting transfers between devices, body(): lax.all_to_all(outgoing_msgs.reshape(peer_count, fetch_slots, width), 'in...  9.03 us
    ppermute x5, starting transfers between devices, body(): earlier = jax.lax.ppermute(all_requests, 'index', k0)  5.93 us
    reduce_sum x1, other arithmetic, body(): jnp.sum(jnp.where(slots[:, :, None] == slot_ids[None, None, :], weights_n...  4.35 us
    dot_general x1, matrix products, body(): jnp.dot(features, w_self, preferred_element_type=jnp.float32)  3.47 us
  transfers between devices with their start and end apart: 6, of which 5 were waited for; matrix products, arithmetic and copies ran while one was open for 8% of the time, Pallas kernels for 0%

profile of v1, /device:TPU:1, one launch (start us, length us, event | category | flops | bytes accessed | tf_op | source)
XLA Modules:
  0.0 129.6 jit_solution(8537769343348493927)
XLA Ops:
  0.0 0.8 convert_bitcast_fusion
  1.1 3.3 %collective-permute-start = (f32[32,32,16]{2,0,1:T(8,128)S(1)}, f32[32,32,16]{2,0,1:T(8,128)S(1)}, u32[]{:S(2)}, u32[]{:S(2)}) collective-permute-start(f32[32,32,16]{2,0,1:T(8,128)S(1)} %broadcast_select_fusion), channel_id=1, source_target_pairs={{0,1},{1,0},{2,3},{3,2},{4,5},{5,4},{6,7},{7,6},{8,9},{9,8},{10,11... | collective-permute-start | bytes 196616 | tf_op jit(solution)/shard_map/ppermute | solution.py:50
  4.4 3.5 %fusion.15 = f32[256,1024]{1,0:T(8,128)} fusion(bf16[256,1024]{1,0:T(8,128)(2,1)} %param.11, bf16[1024,1024]{1,0:T(8,128)(2,1)} %param.14), kind=kOutput, calls=%fused_computation.39 | convolution fusion | flops 536870912 | bytes 3670016 | tf_op jit(solution)/shard_map/dot_general | solution.py:76
  8.1 1.5 %fusion.3 = bf16[256,1024]{1,0:T(8,128)(2,1)} fusion(bf16[256,1024]{1,0:T(8,128)(2,1)S(1)} %copy-done.2, bf16[1024,1024]{1,0:T(8,128)(2,1)S(1)} %copy-done.6, f32[1024]{0:T(1024)S(1)} %copy-done.8), kind=kOutput, calls=%fused_computation.9 | convolution fusion | flops 537657344 | bytes 3149824 | tf_op jit(solution)/shard_map/dot_general | solution.py:54
  9.7 11.8 %collective-permute-done.1 = f32[32,32,16]{2,0,1:T(8,128)S(1)} collective-permute-done((f32[32,32,16]{2,0,1:T(8,128)S(1)}, f32[32,32,16]{2,0,1:T(8,128)S(1)}, u32[]{:S(2)}, u32[]{:S(2)}) %collective-permute-start.1) | collective-permute-done | bytes 65568 | tf_op jit(solution)/shard_map/ppermute | solution.py:50
  21.4 0.2 fusion.27
  21.6 1.3 %collective-permute-start.2 = (f32[32,32,16]{2,0,1:T(8,128)S(1)}, f32[32,32,16]{2,0,1:T(8,128)}, u32[]{:S(2)}, u32[]{:S(2)}) collective-permute-start(f32[32,32,16]{2,0,1:T(8,128)S(1)} %fusion.27), channel_id=1, source_target_pairs={{0,4},{1,5},{2,6},{3,7},{4,0},{5,1},{6,2},{7,3},{8,12},{9,13},{10,... | collective-permute-start | bytes 196616 | tf_op jit(solution)/shard_map/ppermute | solution.py:50
  22.9 0.6 reduce-window.6
  23.5 12.3 %collective-permute-done.2 = f32[32,32,16]{2,0,1:T(8,128)} collective-permute-done((f32[32,32,16]{2,0,1:T(8,128)S(1)}, f32[32,32,16]{2,0,1:T(8,128)}, u32[]{:S(2)}, u32[]{:S(2)}) %collective-permute-start.2) | collective-permute-done | bytes 65568 | tf_op jit(solution)/shard_map/ppermute | solution.py:50
  35.8 1.1 add.59
  37.0 0.2 slice_reduce_fusion
  37.2 11.4 %collective-permute-done.3 = f32[32,32,16]{2,0,1:T(8,128)S(1)} collective-permute-done((f32[32,32,16]{2,0,1:T(8,128)S(1)}, f32[32,32,16]{2,0,1:T(8,128)S(1)}, u32[]{:S(2)}, u32[]{:S(2)}) %collective-permute-start.3) | collective-permute-done | bytes 65568 | tf_op jit(solution)/shard_map/ppermute | solution.py:50
  48.7 1.1 collective-permute-start.4
  50.0 11.1 %collective-permute-done.4 = f32[32,32,16]{2,0,1:T(8,128)S(1)} collective-permute-done((f32[32,32,16]{2,0,1:T(8,128)S(1)}, f32[32,32,16]{2,0,1:T(8,128)S(1)}, u32[]{:S(2)}, u32[]{:S(2)}) %collective-permute-start.4) | collective-permute-done | bytes 65568 | tf_op jit(solution)/shard_map/ppermute | solution.py:50
  61.2 2.6 %convolution_convert_fusion.1 = bf16[512,1024]{1,0:T(8,128)(2,1)} fusion(bf16[256,1024]{1,0:T(8,128)(2,1)} %fusion.3, s32[512]{0:T(512)S(1)} %convert_element_type.48), kind=kOutput, calls=%fused_computation.3 | convolution fusion | flops 269090816 | bytes 1574912 | tf_op jit(solution)/shard_map/dot_general | solution.py:62
  63.8 9.0 %all-to-all-start = ((bf16[32,16,1024]{2,1,0:T(8,128)(2,1)}), bf16[32,16,1024]{2,1,0:T(8,128)(2,1)}, u32[]{:S(2)}, u32[]{:S(2)}) async-start(bf16[32,16,1024]{2,1,0:T(8,128)(2,1)} %bitcast.6), calls=%async_computation | async-start | bytes 2097152 | tf_op jit(solution)/shard_map/all_to_all | solution.py:67
  72.9 4.3 %select_reduce_fusion = bf16[256,512]{1,0:T(8,128)(2,1)S(1)} fusion(f32[256,50]{0,1:T(8,128)S(1)} %broadcast_divide_fusion, s32[256,50]{0,1:T(8,128)S(1)} %copy-done.4), kind=kLoop, calls=%fused_computation | loop fusion | flops 19529728 | bytes 364544 | tf_op jit(solution)/shard_map/reduce_sum | solution.py:58
  77.2 12.5 %all-to-all-done = bf16[32,16,1024]{2,1,0:T(8,128)(2,1)} async-done(((bf16[32,16,1024]{2,1,0:T(8,128)(2,1)}), bf16[32,16,1024]{2,1,0:T(8,128)(2,1)}, u32[]{:S(2)}, u32[]{:S(2)}) %all-to-all-start) | async-done | bytes 1048608 | tf_op jit(solution)/shard_map/all_to_all | solution.py:67
  89.8 3.2 %multiply_reduce_fusion = (f32[256]{0:T(256)S(1)}, f32[256,1024]{1,0:T(8,128)}) fusion(f32[1024]{0:T(1024)S(1)} %copy-done.9, f32[256,1024]{1,0:T(8,128)S(1)} %copy-done.1, bf16[1024,1024]{1,0:T(8,128)(2,1)S(1)} %copy-done, bf16[512,1024]{1,0:T(8,128)(2,1)} %bitcast.7, bf16[256,512]{1,0:T(8,128)(2,1)S(1)} %select_reduce_fusion), kind=kOutput, calls=%fused_computation.14 | convolution fusion | flops 806878976 | bytes 5510144 | tf_op jit(solution)/shard_map/dot_general | solution.py:77
  93.0 1.8 %convolution_convert_fusion = bf16[512,1024]{1,0:T(8,128)(2,1)S(1)} fusion(f32[256,1024]{1,0:T(8,128)} %get-tuple-element.6, f32[256]{0:T(256)S(1)} %add_rsqrt_fusion, s32[256]{0:T(256)S(1)} %bitcast.46), kind=kOutput, calls=%fused_computation.2 | convolution fusion | flops 269615104 | bytes 2099200 | tf_op jit(solution)/shard_map/dot_general | solution.py:85
  94.9 20.6 %all_to_all.15 = bf16[32,16,1024]{2,1,0:T(8,128)(2,1)S(1)} all-to-all(bf16[32,16,1024]{2,1,0:T(8,128)(2,1)S(1)} %bitcast.40), channel_id=1, replica_groups=mesh['graph'=8,'index'=32] {'index'}, dimensions={0} | all-to-all | bytes 2097152 | tf_op jit(solution)/shard_map/all_to_all | solution.py:89
  115.5 0.5 convolution_convert_fusion.3
  116.0 12.7 %all_to_all.16 = bf16[32,16,256]{2,1,0:T(8,128)(2,1)S(1)} all-to-all(bf16[32,16,256]{2,1,0:T(8,128)(2,1)S(1)} %bitcast.43), channel_id=1, replica_groups=mesh['graph'=8,'index'=32] {'index'}, dimensions={0} | all-to-all | bytes 524288 | tf_op jit(solution)/shard_map/all_to_all | solution.py:94
  128.7 0.9 convolution_convert_fusion.4
  (38 shorter events, 0.9 us)
Async XLA Ops:
  0.0 89.8 %copy-start = (bf16[1024,1024]{1,0:T(8,128)(2,1)S(1)}, bf16[1024,1024]{1,0:T(8,128)(2,1)}, u32[]{:S(2)}) copy-start(bf16[1024,1024]{1,0:T(8,128)(2,1)} %param.15) | copy-start | bytes 6291460
  1.1 7.0 %copy-start.2 = (bf16[256,1024]{1,0:T(8,128)(2,1)S(1)}, bf16[256,1024]{1,0:T(8,128)(2,1)}, u32[]{:S(2)}) copy-start(bf16[256,1024]{1,0:T(8,128)(2,1)} %param.11) | copy-start | bytes 1572868
  1.1 7.0 %copy-start.6 = (bf16[1024,1024]{1,0:T(8,128)(2,1)S(1)}, bf16[1024,1024]{1,0:T(8,128)(2,1)}, u32[]{:S(2)}) copy-start(bf16[1024,1024]{1,0:T(8,128)(2,1)} %param.12) | copy-start | bytes 6291460
  1.1 7.0 %copy-start.8 = (f32[1024]{0:T(1024)S(1)}, f32[1024]{0:T(1024)}, u32[]{:S(2)}) copy-start(f32[1024]{0:T(1024)} %param.13) | copy-start | bytes 12292
  1.1 6.8 %collective-permute-start = (f32[32,32,16]{2,0,1:T(8,128)S(1)}, f32[32,32,16]{2,0,1:T(8,128)S(1)}, u32[]{:S(2)}, u32[]{:S(2)}) collective-permute-start(f32[32,32,16]{2,0,1:T(8,128)S(1)} %broadcast_select_fusion), channel_id=1, source_target_pairs={{0,1},{1,0},{2,3},{3,2},{4,5},{5,4},{6,7},{7,6},{8,9},{9,8},{10,11... | collective-permute-start | bytes 196616 | tf_op jit(solution)/shard_map/ppermute | solution.py:50
  8.0 14.9 %copy-start.5 = (s32[256,1]{0,1:T(1,128)S(1)}, s32[256,1]{0,1:T(1,128)}, u32[]{:S(2)}) copy-start(s32[256,1]{0,1:T(1,128)} %param.21) | copy-start | bytes 3076
  8.0 13.4 %collective-permute-start.1 = (f32[32,32,16]{2,0,1:T(8,128)S(1)}, f32[32,32,16]{2,0,1:T(8,128)S(1)}, u32[]{:S(2)}, u32[]{:S(2)}) collective-permute-start(f32[32,32,16]{2,0,1:T(8,128)S(1)} %fusion.10), channel_id=1, source_target_pairs={{0,2},{1,3},{2,0},{3,1},{4,6},{5,7},{6,4},{7,5},{8,10},{9,11},{10,... | collective-permute-start | bytes 196616 | tf_op jit(solution)/shard_map/ppermute | solution.py:50
  21.6 14.2 %collective-permute-start.2 = (f32[32,32,16]{2,0,1:T(8,128)S(1)}, f32[32,32,16]{2,0,1:T(8,128)}, u32[]{:S(2)}, u32[]{:S(2)}) collective-permute-start(f32[32,32,16]{2,0,1:T(8,128)S(1)} %fusion.27), channel_id=1, source_target_pairs={{0,4},{1,5},{2,6},{3,7},{4,0},{5,1},{6,2},{7,3},{8,12},{9,13},{10,... | collective-permute-start | bytes 196616 | tf_op jit(solution)/shard_map/ppermute | solution.py:50
  36.9 11.7 %collective-permute-start.3 = (f32[32,32,16]{2,0,1:T(8,128)S(1)}, f32[32,32,16]{2,0,1:T(8,128)S(1)}, u32[]{:S(2)}, u32[]{:S(2)}) collective-permute-start(f32[32,32,16]{2,0,1:T(8,128)S(1)} %add.59), channel_id=1, source_target_pairs={{0,8},{1,9},{2,10},{3,11},{4,12},{5,13},{6,14},{7,15},{8,0},{9,1},... | collective-permute-start | bytes 196616 | tf_op jit(solution)/shard_map/ppermute | solution.py:50
  48.7 24.1 %copy-start.3 = (f32[256,50]{0,1:T(8,128)S(1)}, f32[256,50]{0,1:T(8,128)}, u32[]{:S(2)}) copy-start(f32[256,50]{0,1:T(8,128)} %param.20) | copy-start | bytes 153604
  48.7 24.2 %copy-start.4 = (s32[256,50]{0,1:T(8,128)S(1)}, s32[256,50]{0,1:T(8,128)}, u32[]{:S(2)}) copy-start(s32[256,50]{0,1:T(8,128)} %param.19) | copy-start | bytes 153604
  48.7 12.4 %collective-permute-start.4 = (f32[32,32,16]{2,0,1:T(8,128)S(1)}, f32[32,32,16]{2,0,1:T(8,128)S(1)}, u32[]{:S(2)}, u32[]{:S(2)}) collective-permute-start(f32[32,32,16]{2,0,1:T(8,128)S(1)} %add.60), channel_id=1, source_target_pairs={{0,16},{1,17},{2,18},{3,19},{4,20},{5,21},{6,22},{7,23},{8,24},{9,... | collective-permute-start | bytes 196616 | tf_op jit(solution)/shard_map/ppermute | solution.py:50
  61.2 28.6 %copy-start.1 = (f32[256,1024]{1,0:T(8,128)S(1)}, f32[256,1024]{1,0:T(8,128)}, u32[]{:S(2)}) copy-start(f32[256,1024]{1,0:T(8,128)} %fusion.15) | copy-start | bytes 3145732
  61.2 28.6 %copy-start.9 = (f32[1024]{0:T(1024)S(1)}, f32[1024]{0:T(1024)}, u32[]{:S(2)}) copy-start(f32[1024]{0:T(1024)} %param.16) | copy-start | bytes 12292
  63.8 26.0 %all-to-all-start = ((bf16[32,16,1024]{2,1,0:T(8,128)(2,1)}), bf16[32,16,1024]{2,1,0:T(8,128)(2,1)}, u32[]{:S(2)}, u32[]{:S(2)}) async-start(bf16[32,16,1024]{2,1,0:T(8,128)(2,1)} %bitcast.6), calls=%async_computation | async-start | bytes 2097152 | tf_op jit(solution)/shard_map/all_to_all | solution.py:67
  93.0 22.5 %copy-start.7 = (bf16[256,1024]{1,0:T(8,128)(2,1)S(1)}, bf16[256,1024]{1,0:T(8,128)(2,1)}, u32[]{:S(2)}) copy-start(bf16[256,1024]{1,0:T(8,128)(2,1)} %param.17) | copy-start | bytes 1572868
